TPU v7x, 32 devices: a whole 2x2x4 slice. The times are simulated.
32 devices in a mesh: lon: 4 (over x, core), lat: 8 (over z, y).
Axes of the slice: x: 2, y: 2, z: 4, core: 2. Of those that a mesh axis runs over, the one named last changes fastest.
Arguments:
- prognostic: float32 [4, 16, 192, 1536], P(None, None, 'lat', 'lon'), may hold values from -6 to 6
- tracers: float32 [4, 16, 192, 1536], P(None, None, 'lat', 'lon'), may hold values from -6 to 6
- zonal_courant: float32 [16, 192, 1536], P(None, 'lat', 'lon'), may hold values from -0.45 to 0.45
- meridional_courant: float32 [16, 192, 1536], P(None, 'lat', 'lon'), may hold values from -0.45 to 0.45
- filter_band: int32 [192], P('lat'), may hold values from 96 to 768, as said below
- dep_owner: int32 [192, 2], P('lat'), may hold values from 0 to 7, as said below
- dep_row: int32 [192, 2], P('lat'), may hold values from 0 to 23
- dep_weight: float32 [192, 2], P('lat'), may hold values from 0 to 1, as said below
Outputs:
- new_prognostic: float32 [4, 16, 192, 1536], P(None, None, 'lat', 'lon')
- new_tracers: float32 [4, 16, 192, 1536], P(None, None, 'lat', 'lon')
Inputs may be any that keep to these rules, and one draw needn't show every extreme that they name: `filter_band`: rows within 24 of either pole hold values below 768; all other rows hold 768. `dep_owner`: among the 48 entries of one band, at most 12 name the same owner band, and some owner is named exactly 12 times; the owners a band names are the bands nearest to it, distance counted across either pole. `dep_weight`: Positive; the 2 weights of a row sum to 1.
All inputs are finite; a program needn't handle non-finite values.
Results may differ from a plain program's by a relative error of at most 0.00007.
Values sent between devices are 32-bit elements; how exact they have to be, the bound alone decides.
No kernel may reach another device: no remote copies, remote signals or barrier semaphores. Data moves between devices by JAX's collectives and lax.ppermute only.
A program may use at most 128 MiB of HBM per device.

v0:
```python
import math

import jax
import jax.numpy as jnp
from jax import lax
from jax.sharding import PartitionSpec as P

PRECISE = lax.Precision.HIGHEST


def padded(value, sides, width, wrap):
    for axis, dim in sides:
        size, length = (lax.axis_size(axis), value.shape[dim])
        up = [(i, (i + 1) % size) for i in range(size if wrap else size - 1)]
        down = [(j, i) for i, j in up]
        last = lax.slice_in_dim(value, length - width, length, axis=dim)
        first = lax.slice_in_dim(value, 0, width, axis=dim)
        before = lax.ppermute(last, axis, up)
        after = lax.ppermute(first, axis, down)
        value = jnp.concatenate([before, value, after], axis=dim)
    return value


def face_flux(values, speeds, axis):
    count = values.shape[axis] - 2
    left_cells = lax.slice_in_dim(values, 0, count + 1, axis=axis)
    right_cells = lax.slice_in_dim(values, 1, count + 2, axis=axis)
    courant = lax.slice_in_dim(speeds, 0, count + 1, axis=axis)
    return 0.5 * courant * (left_cells + right_cells) - 0.5 * courant * courant * (
        right_cells - left_cells
    )


def real_basis(first_cell, count, length):
    cells = first_cell + jnp.arange(count, dtype=jnp.int32)
    column = jnp.arange(length, dtype=jnp.int32)
    half_length = length // 2
    frequency = jnp.where(column <= half_length, column, column - half_length)
    phase_index = cells[:, None] * frequency[None, :] % length
    angles = 2.0 * math.pi / length * phase_index.astype(jnp.float32)
    return jnp.where((column <= half_length)[None, :], jnp.cos(angles), jnp.sin(angles))


def column_factors(band_rows, length):
    column = jnp.arange(length, dtype=jnp.int32)
    half_length = length // 2
    frequency = jnp.where(column <= half_length, column, column - half_length)
    single = (column == 0) | (column == half_length)
    weights = jnp.where(single, 1.0 / length, 2.0 / length).astype(jnp.float32)
    ratios = (
        band_rows.astype(jnp.float32)[:, None]
        / jnp.maximum(frequency, 1).astype(jnp.float32)[None, :]
    )
    damping = jnp.minimum(1.0, ratios * ratios)
    return (damping - 1.0) * weights[None, :]


def polar_filter(values, band_rows):
    block_cells = values.shape[3]
    length = block_cells * lax.axis_size("lon")
    basis_table = real_basis(lax.axis_index("lon") * block_cells, block_cells, length)
    needed = jnp.any(band_rows < length // 2)

    def forward(grid):
        return jnp.einsum("flrn,nk->flrk", grid, basis_table, precision=PRECISE)

    def nothing(grid):
        return jnp.zeros(grid.shape[:3] + (length,), jnp.float32)

    partial_spec = lax.cond(needed, forward, nothing, values)
    spectrum = lax.psum(partial_spec, "lon")
    factors = column_factors(band_rows, length)

    def inverse(coeffs):
        return jnp.einsum(
            "flrk,nk->flrn", coeffs * factors[None, None], basis_table, precision=PRECISE
        )

    def no_change(coeffs):
        return jnp.zeros(coeffs.shape[:3] + (block_cells,), jnp.float32)

    return values + lax.cond(needed, inverse, no_change, spectrum)


def departure_terms(tracers, dep_owner, dep_row, dep_weight):
    band_count = lax.axis_size("lat")
    row_count, link_count = dep_owner.shape
    entries = row_count * link_count
    capacity = max(2, -(-2 * entries // band_count))
    owner_ids = dep_owner.reshape(entries)
    source = dep_row.reshape(entries)
    positions = jnp.arange(entries)
    earlier = (owner_ids[:, None] == owner_ids[None, :]) & (positions[None, :] < positions[:, None])
    slot_ids = jnp.sum(earlier.astype(jnp.int32), axis=1)
    band_ids = jnp.arange(band_count, dtype=jnp.int32)
    slot_range = jnp.arange(capacity, dtype=jnp.int32)
    matches = (owner_ids[:, None, None] == band_ids[None, :, None]) & (
        slot_ids[:, None, None] == slot_range[None, None, :]
    )
    request = jnp.sum(jnp.where(matches, source[:, None, None], 0), axis=0)
    wanted = lax.all_to_all(request, "lat", split_axis=0, concat_axis=0, tiled=True)
    by_row = jnp.transpose(tracers, (2, 0, 1, 3))
    outgoing = by_row[wanted]
    incoming = lax.all_to_all(outgoing, "lat", split_axis=0, concat_axis=0, tiled=True)
    stacked_rows = incoming.reshape((band_count * capacity,) + incoming.shape[2:])
    picked = stacked_rows[owner_ids * capacity + slot_ids].reshape(
        (row_count, link_count) + stacked_rows.shape[1:]
    )
    summed = dep_weight[:, 0][:, None, None, None] * picked[:, 0]
    summed = summed + dep_weight[:, 1][:, None, None, None] * picked[:, 1]
    return jnp.transpose(summed, (1, 2, 0, 3))


def body(
    prognostic,
    tracers,
    zonal_courant,
    meridional_courant,
    filter_band,
    dep_owner,
    dep_row,
    dep_weight,
):
    row_count = prognostic.shape[2]
    departed = departure_terms(tracers, dep_owner, dep_row, dep_weight)
    lon_padded = padded(
        jnp.concatenate([prognostic, zonal_courant[None]], axis=0), (("lon", 3),), 1, True
    )
    zonal_flux = face_flux(lon_padded[:-1], lon_padded[-1:], 3)
    lat_padded = padded(
        jnp.concatenate([prognostic, meridional_courant[None]], axis=0), (("lat", 2),), 1, False
    )
    merid_flux = face_flux(lat_padded[:-1], lat_padded[-1:], 2)
    total_rows = row_count * lax.axis_size("lat")
    face_rows = lax.axis_index("lat") * row_count + jnp.arange(row_count + 1) - 1
    merid_flux = jnp.where(
        (face_rows == total_rows - 1)[None, None, :, None], jnp.float32(0.0), merid_flux
    )
    advected = (
        prognostic
        - (zonal_flux[..., 1:] - zonal_flux[..., :-1])
        - (merid_flux[:, :, 1:] - merid_flux[:, :, :-1])
    )
    new_prognostic = polar_filter(advected, filter_band)
    return (new_prognostic, departed)


def solution(mesh):
    return jax.shard_map(
        body,
        mesh=mesh,
        in_specs=(
            P(None, None, "lat", "lon"),
            P(None, None, "lat", "lon"),
            P(None, "lat", "lon"),
            P(None, "lat", "lon"),
            P("lat"),
            P("lat", None),
            P("lat", None),
            P("lat", None),
        ),
        out_specs=(P(None, None, "lat", "lon"), P(None, None, "lat", "lon")),
        check_vma=False,
    )
```

profile of v0, /device:TPU:0, one launch (start us, length us, event | category | flops | bytes accessed | tf_op | source)
XLA Modules:
  0.0 461.9 jit_solution(5204649697896423825)
XLA Ops:
  7.2 0.8 copy.66
  8.2 0.8 copy.67
  9.4 0.7 copy.69
  10.1 7.3 %all-to-all-start = ((s32[8,1,12]{2,1,0:T(1,128)}), s32[8,1,12]{2,1,0:T(1,128)S(1)}, u32[]{:S(2)}, u32[]{:S(2)}) async-start(s32[8,1,12]{2,1,0:T(1,128)} %copy.69), calls=%async_computation | async-start | bytes 8192 | tf_op jit(solution)/shard_map/all_to_all | solution.py:101
  17.3 2.1 copy.83
  19.5 4.3 all-to-all-done
  23.8 4.8 %gather_fusion = f32[96,4,16,384]{3,2,1,0:T(8,128)} fusion(f32[24,4,16,384]{3,2,1,0:T(8,128)S(1)} %bitcast.59, s32[1024]{0:T(1024)S(1)} %pad_clamp_fusion.1), kind=kCustom, calls=%fused_computation | custom fusion | bytes 18874752 | tf_op jit(solution)/shard_map/gather | solution.py:103
  28.6 5.3 %all-to-all-start.1 = ((f32[8,12,4,16,384]{4,3,2,1,0:T(8,128)}), f32[8,12,4,16,384]{4,3,2,1,0:T(8,128)}, u32[]{:S(2)}, u32[]{:S(2)}) async-start(f32[8,12,4,16,384]{4,3,2,1,0:T(8,128)} %bitcast.60), calls=%async_computation.1 | async-start | bytes 18874368 | tf_op jit(solution)/shard_map/all_to_all | solution.py:104
  34.2 4.4 collective-permute-start.2
  39.3 1.3 collective-permute-start.3
  40.6 1.6 pad_maximum_fusion.8
  42.1 1.7 copy.77
  43.9 1.7 copy.78
  45.6 1.8 collective-permute-start.1
  48.1 10.9 %sine_select_fusion = f32[384,1536]{1,0:T(8,128)} fusion(s32[1536]{0:T(1024)S(1)} %add_select_fusion.1, s32[384]{0:T(512)S(1)} %iota_add_fusion, pred[1536]{0:T(1024)(128)(4,1)S(1)} %iota_compare_fusion.2), kind=kLoop, calls=%fused_computation.42 | loop fusion | flops 5898240 | bytes 2368512 | tf_op jit(solution)/shard_map/jit(_where)/select_n | solution.py:41
  60.1 2.3 copy.60
  62.4 1.5 multiply_bitcast_fusion.1
  64.0 1.5 multiply_subtract_fusion
  65.4 49.1 %collective-permute-done.2 = f32[5,16,1,384]{3,1,2,0:T(8,128)} collective-permute-done((f32[5,16,1,384]{3,1,2,0:T(8,128)S(1)}, f32[5,16,1,384]{3,1,2,0:T(8,128)}, u32[]{:S(2)}, u32[]{:S(2)}) %collective-permute-start.2) | collective-permute-done | bytes 122912 | tf_op jit(solution)/shard_map/ppermute | solution.py:18
  114.5 1.0 copy.62
  115.6 1.0 copy.64
  116.9 1.2 subtract_select_fusion
  118.0 2.3 fusion.16
  120.3 20.0 %conditional.2 = (f32[4,16,24,1536]{3,2,1,0:T(8,128)}) conditional(s32[]{:T(128)} %convert_element_type.23, () %tuple.57, (f32[4,16,24,384]{3,2,1,0:T(8,128)}, f32[384,1536]{1,0:T(8,128)}) %tuple.58), branch_computations={%region_1.2_spmd, %region_2.3_spmd} | conditional | flops 10871635968 | bytes 14155784 | solution.py:70
  120.3 20.0 %fusion = f32[4,16,24,1536]{3,2,1,0:T(8,128)} fusion(f32[4,16,24,384]{3,2,1,0:T(8,128)} %get-tuple-element.63, f32[384,1536]{1,0:T(8,128)} %get-tuple-element.64), kind=kOutput, calls=%fused_computation.2 | convolution fusion | flops 10871635968 | bytes 14155776 | tf_op jit(solution)/shard_map/cond/branch_1_fun/flrn,nk->flrk/dot_general | solution.py:65
  141.2 278.5 %all-reduce.2.cloned.1.call-done = f32[4,16,24,1536]{3,2,1,0:T(8,128)} async-done(((f32[4,16,24,1536]{3,2,1,0:T(8,128)}), f32[4,16,24,1536]{3,2,1,0:T(8,128)}) %all-reduce.2.cloned.1.call-update) | async-done | bytes 9437200 | tf_op jit(solution)/shard_map/psum | solution.py:71
  419.8 19.6 %conditional.3 = (f32[4,16,24,384]{3,2,1,0:T(8,128)}) conditional(s32[]{:T(128)} %convert_element_type.23, () %tuple.56, (f32[24]{0:T(128)S(1)}, f32[1,1536]{1,0:T(1,128)S(1)}, s32[1,1536]{1,0:T(1,128)S(1)}, s32[1,1536]{1,0:T(1,128)S(1)}, f32[4,16,24,1536]{3,2,1,0:T(8,128)}, /*index=5*/f32[384,1536]{1,0:T(8,128)}) %tuple.59), branch_computations={%region_4.5_spmd, %region_5.6_spmd} | conditional | flops 10874185728 | bytes 14493804 | solution.py:82
  420.2 19.2 %fusion.2 = f32[4,16,24,384]{3,2,1,0:T(8,128)} fusion(f32[4,16,24,1536]{3,2,1,0:T(8,128)} %get-tuple-element.65, f32[24,1536]{1,0:T(8,128)S(1)} %fusion.8, f32[384,1536]{1,0:T(8,128)} %get-tuple-element.70), kind=kOutput, calls=%fused_computation.4 | convolution fusion | flops 10873995264 | bytes 14303232 | tf_op jit(solution)/shard_map/cond/branch_1_fun/flrk,nk->flrn/dot_general | solution.py:75
  439.3 3.3 add.102
  442.6 6.8 %gather_fusion.1 = f32[48,4,16,384]{3,2,1,0:T(8,128)} fusion(f32[96,4,16,384]{3,2,1,0:T(8,128)} %bitcast.15, s32[1024]{0:T(1024)S(1)} %pad_clamp_fusion), kind=kCustom, calls=%fused_computation.1 | custom fusion | bytes 9437376 | tf_op jit(solution)/shard_map/gather | solution.py:106
  449.4 2.9 fusion.14
  452.3 2.8 copy.72
  (63 shorter events, 4.3 us)
Async XLA Ops:
  10.1 13.7 %all-to-all-start = ((s32[8,1,12]{2,1,0:T(1,128)}), s32[8,1,12]{2,1,0:T(1,128)S(1)}, u32[]{:S(2)}, u32[]{:S(2)}) async-start(s32[8,1,12]{2,1,0:T(1,128)} %copy.69), calls=%async_computation | async-start | bytes 8192 | tf_op jit(solution)/shard_map/all_to_all | solution.py:101
  28.6 5.4 %copy-start = (f32[4,16,24,384]{3,2,1,0:T(8,128)S(1)}, f32[4,16,24,384]{3,2,1,0:T(8,128)}, u32[]{:S(2)}) copy-start(f32[4,16,24,384]{3,2,1,0:T(8,128)} %param.12) | copy-start | bytes 7077892
  28.6 5.4 %copy-start.4 = (f32[16,24,384]{2,1,0:T(8,128)S(1)}, f32[16,24,384]{2,1,0:T(8,128)}, u32[]{:S(2)}) copy-start(f32[16,24,384]{2,1,0:T(8,128)} %param.15) | copy-start | bytes 1769476
  28.6 414.0 %all-to-all-start.1 = ((f32[8,12,4,16,384]{4,3,2,1,0:T(8,128)}), f32[8,12,4,16,384]{4,3,2,1,0:T(8,128)}, u32[]{:S(2)}, u32[]{:S(2)}) async-start(f32[8,12,4,16,384]{4,3,2,1,0:T(8,128)} %bitcast.60), calls=%async_computation.1 | async-start | bytes 18874368 | tf_op jit(solution)/shard_map/all_to_all | solution.py:104
  33.9 6.6 %copy-start.2 = (f32[16,24,384]{2,1,0:T(8,128)S(1)}, f32[16,24,384]{2,1,0:T(8,128)}, u32[]{:S(2)}) copy-start(f32[16,24,384]{2,1,0:T(8,128)} %param.14) | copy-start | bytes 1769476
  34.0 385.8 %all-reduce.2.cloned.1.call-start = ((), (), s32[]{:S(2)}) async-start(), calls=%async_computation.2 | async-start | bytes 18874368 | tf_op jit(solution)/shard_map/psum | solution.py:71
  34.2 80.3 %collective-permute-start.2 = (f32[5,16,1,384]{3,1,2,0:T(8,128)S(1)}, f32[5,16,1,384]{3,1,2,0:T(8,128)}, u32[]{:S(2)}, u32[]{:S(2)}) collective-permute-start(f32[5,16,1,384]{3,1,2,0:T(8,128)S(1)} %copy.79), channel_id=1, source_target_pairs={{0,1},{1,2},{2,3},{3,4},{4,5},{5,6},{6,7},{8,9},{9,10},{10,11},{11... | collective-permute-start | bytes 368648 | tf_op jit(solution)/shard_map/ppermute | solution.py:18
  39.3 76.3 %collective-permute-start.3 = (f32[5,16,1,384]{3,1,2,0:T(8,128)}, f32[5,16,1,384]{3,1,2,0:T(8,128)}, u32[]{:S(2)}, u32[]{:S(2)}) collective-permute-start(f32[5,16,1,384]{3,1,2,0:T(8,128)} %copy.80), channel_id=1, source_target_pairs={{1,0},{2,1},{3,2},{4,3},{5,4},{6,5},{7,6},{9,8},{10,9},{11,10},{12... | collective-permute-start | bytes 368648 | tf_op jit(solution)/shard_map/ppermute | solution.py:19
  40.6 6.9 %copy-start.9 = (s32[24]{0:T(128)S(1)}, s32[24]{0:T(128)}, u32[]{:S(2)}) copy-start(s32[24]{0:T(128)} %param.16) | copy-start | bytes 292
  43.9 15.7 %collective-permute-start = (f32[5,16,24,1]{2,1,3,0:T(8,128)S(1)}, f32[5,16,24,1]{2,1,3,0:T(8,128)S(1)}, u32[]{:S(2)}, u32[]{:S(2)}) collective-permute-start(f32[5,16,24,1]{2,1,3,0:T(8,128)S(1)} %copy.77), channel_id=1, source_target_pairs={{0,8},{8,16},{16,24},{24,0},{1,9},{9,17},{17,25},{25,1},{2,10},{10... | collective-permute-start | bytes 23048 | tf_op jit(solution)/shard_map/ppermute | solution.py:18
  45.6 14.5 %collective-permute-start.1 = (f32[5,16,24,1]{2,1,3,0:T(8,128)S(1)}, f32[5,16,24,1]{2,1,3,0:T(8,128)}, u32[]{:S(2)}, u32[]{:S(2)}) collective-permute-start(f32[5,16,24,1]{2,1,3,0:T(8,128)S(1)} %copy.78), channel_id=1, source_target_pairs={{8,0},{16,8},{24,16},{0,24},{9,1},{17,9},{25,17},{1,25},{10,2},{18... | collective-permute-start | bytes 23048 | tf_op jit(solution)/shard_map/ppermute | solution.py:19
  62.4 1.6 copy-start.3
  62.4 1.6 copy-start.6
  64.0 52.6 %copy-start.5 = (f32[16,24,384]{2,1,0:T(8,128)S(1)}, f32[16,24,384]{2,1,0:T(8,128)}, u32[]{:S(2)}) copy-start(f32[16,24,384]{2,1,0:T(8,128)} %param.15) | copy-start | bytes 1769476
  140.3 0.7 copy-start.10
  140.3 0.7 copy-start.7
  140.3 0.9 copy-start.8
  419.8 19.6 %copy-start.1 = (f32[4,16,24,384]{3,2,1,0:T(8,128)S(1)}, f32[4,16,24,384]{3,2,1,0:T(8,128)}, u32[]{:S(2)}) copy-start(f32[4,16,24,384]{3,2,1,0:T(8,128)} %fusion.16) | copy-start | bytes 7077892
Sparse Core Ops, SparseCore 0:
  140.4 279.2 all-reduce.1
where the time goes:
time: 463 us; the launch traced here: 462 us
  waiting for transfers between devices  332 us (72%)
  matrix products  39.1 us (8%)
  local copies, waits for them, and re-layouts  28.8 us (6%)
  other arithmetic  26.8 us (6%)
  starting transfers between devices  20.1 us (4%)
  between operations  15 us (3%)
    psum x1, waiting for transfers between devices, polar_filter(): spectrum = lax.psum(partial_spec, 'lon')  279 us
    ppermute x2, waiting for transfers between devices, padded(): before = lax.ppermute(last, axis, up)  49.1 us
    dot_general x1, matrix products, forward(): return jnp.einsum('flrn,nk->flrk', grid, basis_table, precision=PRECISE)  20 us
    dot_general x1, matrix products, inverse(): jnp.einsum('flrk,nk->flrn', coeffs * factors[None, None], basis_table, pr...  19.2 us
    unnamed x30, local copies, waits for them, and re-layouts  11.2 us
    select_n x1, other arithmetic, real_basis(): jnp.where((column <= half_length)[None, :], jnp.cos(angles), jnp.sin(angl...  10.9 us
  transfers between devices with their start and end apart: 7, of which 3 were waited for; matrix products, arithmetic and copies ran while one was open for 16% of the time, Pallas kernels for 0%

commit v1 on v0

--- a/solution.py
+++ b/solution.py
@@ -31,16 +31,6 @@
     )
 
 
-def real_basis(first_cell, count, length):
-    cells = first_cell + jnp.arange(count, dtype=jnp.int32)
-    column = jnp.arange(length, dtype=jnp.int32)
-    half_length = length // 2
-    frequency = jnp.where(column <= half_length, column, column - half_length)
-    phase_index = cells[:, None] * frequency[None, :] % length
-    angles = 2.0 * math.pi / length * phase_index.astype(jnp.float32)
-    return jnp.where((column <= half_length)[None, :], jnp.cos(angles), jnp.sin(angles))
-
-
 def column_factors(band_rows, length):
     column = jnp.arange(length, dtype=jnp.int32)
     half_length = length // 2
@@ -55,31 +45,43 @@
     return (damping - 1.0) * weights[None, :]
 
 
+def circle_basis(length):
+    half_length = length // 2
+    column = jnp.arange(length, dtype=jnp.int32)
+    frequency = jnp.where(column <= half_length, column, column - half_length)
+    low_count = 64
+    high_count = length // low_count
+    low = jnp.arange(low_count, dtype=jnp.int32)
+    high = jnp.arange(high_count, dtype=jnp.int32) * low_count
+    scale = 2.0 * math.pi / length
+    low_angle = scale * (low[:, None] * frequency[None, :] % length).astype(jnp.float32)
+    high_angle = scale * (high[:, None] * frequency[None, :] % length).astype(jnp.float32)
+    low_cos, low_sin = jnp.cos(low_angle), jnp.sin(low_angle)
+    high_cos, high_sin = jnp.cos(high_angle), jnp.sin(high_angle)
+    cos_part = high_cos[:, None] * low_cos[None] - high_sin[:, None] * low_sin[None]
+    sin_part = high_sin[:, None] * low_cos[None] + high_cos[:, None] * low_sin[None]
+    basis = jnp.where((column <= half_length)[None, None, :], cos_part, sin_part)
+    return basis.reshape(length, length)
+
+
 def polar_filter(values, band_rows):
-    block_cells = values.shape[3]
-    length = block_cells * lax.axis_size("lon")
-    basis_table = real_basis(lax.axis_index("lon") * block_cells, block_cells, length)
-    needed = jnp.any(band_rows < length // 2)
-
-    def forward(grid):
-        return jnp.einsum("flrn,nk->flrk", grid, basis_table, precision=PRECISE)
-
-    def nothing(grid):
-        return jnp.zeros(grid.shape[:3] + (length,), jnp.float32)
-
-    partial_spec = lax.cond(needed, forward, nothing, values)
-    spectrum = lax.psum(partial_spec, "lon")
+    fields, levels, rows, block_cells = values.shape
+    parts = lax.axis_size("lon")
+    length = block_cells * parts
+    flat = values.reshape(fields * levels * rows, block_cells)
+    circles = lax.all_to_all(flat, "lon", split_axis=0, concat_axis=1, tiled=True)
+    basis_table = circle_basis(length)
+    spectrum = jnp.dot(circles, basis_table, precision=PRECISE)
     factors = column_factors(band_rows, length)
-
-    def inverse(coeffs):
-        return jnp.einsum(
-            "flrk,nk->flrn", coeffs * factors[None, None], basis_table, precision=PRECISE
-        )
-
-    def no_change(coeffs):
-        return jnp.zeros(coeffs.shape[:3] + (block_cells,), jnp.float32)
-
-    return values + lax.cond(needed, inverse, no_change, spectrum)
+    circle_rows = circles.shape[0]
+    scaled = (spectrum.reshape(circle_rows // rows, rows, length) * factors[None]).reshape(
+        circle_rows, length
+    )
+    change = lax.dot_general(
+        scaled, basis_table, (((1,), (1,)), ((), ())), precision=PRECISE
+    )
+    back = lax.all_to_all(change, "lon", split_axis=1, concat_axis=0, tiled=True)
+    return values + back.reshape(values.shape)
 
 
 def departure_terms(tracers, dep_owner, dep_row, dep_weight):

time: 463 us -> 365 us (0.79)
  waiting for transfers between devices: 332 us -> 243 us
  between operations: 15 us -> 0.99 us
  matrix products: 39.1 us -> 27.7 us
  starting transfers between devices: 20.1 us -> 30.1 us
  local copies, waits for them, and re-layouts: 28.8 us -> 34.2 us
    psum x1 -> x0, waiting for transfers between devices: 279 us -> none  [polar_filter(): spectrum = lax.psum(partial_spec, 'lon')]
    all_to_all x1, waiting for transfers between devices: 0.01 us -> 202 us  [departure_terms(): lax.all_to_all(outgoing, 'lat', split_axis=0, concat_axis=0, tiled=True)]
    ppermute x2, waiting for transfers between devices: 49.1 us -> 0.01 us  [padded(): before = lax.ppermute(last, axis, up)]
    all_to_all x0 -> x2, waiting for transfers between devices: none -> 41 us  [the longest x1 21.3 us: polar_filter(): lax.all_to_all(change, 'lon', split_axis=1, concat_axis=0, tiled=True)]
    dot_general x2, matrix products: 39.1 us -> 27.7 us  [the longest x1 14.7 us: polar_filter(): spectrum = jnp.dot(circles, basis_table, precision=PRECISE)]
    all_to_all x0 -> x2, starting transfers between devices: none -> 8.41 us  [the longest x1 4.78 us: polar_filter(): lax.all_to_all(change, 'lon', split_axis=1, concat_axis=0, tiled=True)]
    unnamed x30 -> x28, local copies, waits for them, and re-layouts: 11.2 us -> 5.44 us
    select_n x2, other arithmetic: 10.9 us -> 5.83 us  [the longest x1 5.82 us: circle_basis(): jnp.where((column <= half_length)[None, None, :], cos_part, sin_part)]
  transfers between devices with their start and end apart: 7 -> 8, of which waited for: 3 -> 3; matrix products, arithmetic and copies ran while one was open for 16% -> 19% of each run, Pallas kernels for 0% -> 0%
where the time goes in v1:
time: 365 us; the launch traced here: 364 us
  waiting for transfers between devices  243 us (67%)
  local copies, waits for them, and re-layouts  34.2 us (9%)
  starting transfers between devices  30.1 us (8%)
  other arithmetic  28.6 us (8%)
  matrix products  27.7 us (8%)
    all_to_all x1, waiting for transfers between devices, departure_terms(): lax.all_to_all(outgoing, 'lat', split_axis=0, concat_axis=0, tiled=True)  202 us
    all_to_all x1, waiting for transfers between devices, polar_filter(): lax.all_to_all(change, 'lon', split_axis=1, concat_axis=0, tiled=True)  21.3 us
    all_to_all x1, waiting for transfers between devices, polar_filter(): lax.all_to_all(flat, 'lon', split_axis=0, concat_axis=1, tiled=True)  19.7 us
    dot_general x1, matrix products, polar_filter(): spectrum = jnp.dot(circles, basis_table, precision=PRECISE)  14.7 us
    dot_general x1, matrix products, polar_filter(): lax.dot_general(scaled, basis_table, (((1,), (1,)), ((), ())), precision=...  13 us
  transfers between devices with their start and end apart: 8, of which 3 were waited for; matrix products, arithmetic and copies ran while one was open for 19% of the time, Pallas kernels for 0%

profile of v1, /device:TPU:0, one launch (start us, length us, event | category | flops | bytes accessed | tf_op | source)
XLA Modules:
  0.0 364.4 jit_solution(3108932577473310589)
XLA Ops:
  0.7 3.3 pad_maximum_fusion.8
  4.0 1.8 copy.57
  6.2 1.7 copy.59
  7.9 2.0 collective-permute-start.1
  10.8 4.9 %collective-permute-start.2 = (f32[5,16,1,384]{3,1,2,0:T(8,128)}, f32[5,16,1,384]{3,1,2,0:T(8,128)}, u32[]{:S(2)}, u32[]{:S(2)}) collective-permute-start(f32[5,16,1,384]{3,1,2,0:T(8,128)} %copy.61), channel_id=1, source_target_pairs={{0,1},{1,2},{2,3},{3,4},{4,5},{5,6},{6,7},{8,9},{9,10},{10,11},{11... | collective-permute-start | bytes 368648 | tf_op jit(solution)/shard_map/ppermute | solution.py:18
  16.3 1.3 collective-permute-start.3
  19.5 1.3 copy.58
  20.8 2.2 multiply_bitcast_fusion.1
  24.0 2.3 copy.60
  26.3 2.7 multiply_subtract_fusion
  30.4 1.0 copy.64
  31.4 1.2 subtract_select_fusion
  32.6 2.3 fusion.4
  34.9 3.6 all-to-all-start
  39.9 1.6 fusion.14
  41.5 5.8 %add_select_fusion = f32[24,64,1536]{2,1,0:T(8,128)} fusion(f32[64,1536]{1,0:T(8,128)S(1)} %get-tuple-element.21, f32[24,1536]{1,0:T(8,128)S(1)} %get-tuple-element.19, f32[64,1536]{1,0:T(8,128)S(1)} %get-tuple-element.20, f32[24,1536]{1,0:T(8,128)S(1)} %get-tuple-element.18, pred[1536]{0:T(1024)(128)(4,1)S(1)} %iota_compare_fusion.4), kind=kLoop, calls=%fused_computation.2 | loop fusion | flops 16515072 | bytes 10520064 | tf_op jit(solution)/shard_map/jit(_where)/select_n | solution.py:63
  47.3 19.7 %all-to-all-done = f32[4,384,384]{2,1,0:T(8,128)S(1)} async-done(((f32[4,384,384]{2,1,0:T(8,128)}), f32[4,384,384]{2,1,0:T(8,128)S(1)}, u32[]{:S(2)}, u32[]{:S(2)}) %all-to-all-start) | async-done | bytes 2359328 | tf_op jit(solution)/shard_map/all_to_all | solution.py:72
  67.0 6.9 %all-to-all-start.2 = ((s32[8,1,12]{2,1,0:T(1,128)}), s32[8,1,12]{2,1,0:T(1,128)S(1)}, u32[]{:S(2)}, u32[]{:S(2)}) async-start(s32[8,1,12]{2,1,0:T(1,128)} %copy.70), calls=%async_computation.2 | async-start | bytes 8192 | tf_op jit(solution)/shard_map/all_to_all | solution.py:103
  73.9 2.9 copy.65
  76.9 2.7 dot_general.8
  79.6 14.7 %convolution_multiply_fusion = f32[16,24,1536]{2,1,0:T(8,128)S(1)} fusion(f32[16,24,1536]{2,1,0:T(8,128)S(1)} %dot_general.8, f32[1536,1536,1]{1,0,2:T(8,128)} %bitcast.64, f32[24,1536]{1,0:T(8,128)S(1)} %fusion.18), kind=kOutput, calls=%fused_computation.13 | convolution fusion | flops 10872225792 | bytes 14303232 | tf_op jit(solution)/shard_map/dot_general | solution.py:74
  94.3 13.0 %fusion.31 = f32[384,4,384]{2,0,1:T(8,128)} fusion(f32[384,1536,1]{1,0,2:T(8,128)S(1)} %bitcast.71, f32[4,384,1536]{2,1,0:T(8,128)S(1)} %bitcast.65), kind=kOutput, calls=%fused_computation.87 | convolution fusion | flops 10871635968 | bytes 14155776 | tf_op jit(solution)/shard_map/dot_general | solution.py:80
  107.3 4.8 %all-to-all-start.1 = ((f32[384,4,384]{2,0,1:T(8,128)}), f32[384,4,384]{2,0,1:T(8,128)}, u32[]{:S(2)}, u32[]{:S(2)}) async-start(f32[384,4,384]{2,0,1:T(8,128)} %fusion.31), calls=%async_computation.1 | async-start | bytes 4718592 | tf_op jit(solution)/shard_map/all_to_all | solution.py:83
  112.1 2.1 copy.78
  114.3 4.8 %gather_fusion = f32[96,4,16,384]{3,2,1,0:T(8,128)} fusion(f32[24,4,16,384]{3,2,1,0:T(8,128)S(1)} %bitcast.66, s32[1024]{0:T(1024)S(1)} %pad_clamp_fusion.1), kind=kCustom, calls=%fused_computation | custom fusion | bytes 18874752 | tf_op jit(solution)/shard_map/gather | solution.py:105
  119.1 21.3 %all-to-all-done.1 = f32[384,4,384]{2,0,1:T(8,128)} async-done(((f32[384,4,384]{2,0,1:T(8,128)}), f32[384,4,384]{2,0,1:T(8,128)}, u32[]{:S(2)}, u32[]{:S(2)}) %all-to-all-start.1) | async-done | bytes 2359328 | tf_op jit(solution)/shard_map/all_to_all | solution.py:83
  140.4 6.1 %all-to-all-start.3 = ((f32[8,12,4,16,384]{4,3,2,1,0:T(8,128)}), f32[8,12,4,16,384]{4,3,2,1,0:T(8,128)}, u32[]{:S(2)}, u32[]{:S(2)}) async-start(f32[8,12,4,16,384]{4,3,2,1,0:T(8,128)} %bitcast.67), calls=%async_computation.3 | async-start | bytes 18874368 | tf_op jit(solution)/shard_map/all_to_all | solution.py:106
  146.8 3.3 add.134
  150.1 201.9 %all-to-all-done.3 = f32[8,12,4,16,384]{4,3,2,1,0:T(8,128)} async-done(((f32[8,12,4,16,384]{4,3,2,1,0:T(8,128)}), f32[8,12,4,16,384]{4,3,2,1,0:T(8,128)}, u32[]{:S(2)}, u32[]{:S(2)}) %all-to-all-start.3) | async-done | bytes 9437216 | tf_op jit(solution)/shard_map/all_to_all | solution.py:106
  352.0 6.7 %gather_fusion.1 = f32[48,4,16,384]{3,2,1,0:T(8,128)} fusion(f32[96,4,16,384]{3,2,1,0:T(8,128)} %bitcast.20, s32[1024]{0:T(1024)S(1)} %pad_clamp_fusion), kind=kCustom, calls=%fused_computation.1 | custom fusion | bytes 9437376 | tf_op jit(solution)/shard_map/gather | solution.py:108
  358.7 2.9 fusion.2
  361.6 2.8 copy.73
  (64 shorter events, 7.8 us)
Async XLA Ops:
  0.6 9.3 %copy-start = (f32[4,16,24,384]{3,2,1,0:T(8,128)S(1)}, f32[4,16,24,384]{3,2,1,0:T(8,128)}, u32[]{:S(2)}) copy-start(f32[4,16,24,384]{3,2,1,0:T(8,128)} %param.8) | copy-start | bytes 7077892
  0.6 9.3 %copy-start.3 = (f32[16,24,384]{2,1,0:T(8,128)S(1)}, f32[16,24,384]{2,1,0:T(8,128)}, u32[]{:S(2)}) copy-start(f32[16,24,384]{2,1,0:T(8,128)} %param.11) | copy-start | bytes 1769476
  4.0 13.7 %copy-start.5 = (s32[24,2]{0,1:T(2,128)S(1)}, s32[24,2]{0,1:T(2,128)}, u32[]{:S(2)}) copy-start(s32[24,2]{0,1:T(2,128)} %param.13) | copy-start | bytes 580
  4.0 14.1 %copy-start.11 = (s32[24]{0:T(128)S(1)}, s32[24]{0:T(128)}, u32[]{:S(2)}) copy-start(s32[24]{0:T(128)} %param.12) | copy-start | bytes 292
  4.0 14.1 %copy-start.7 = (s32[24,2]{0,1:T(2,128)S(1)}, s32[24,2]{0,1:T(2,128)}, u32[]{:S(2)}) copy-start(s32[24,2]{0,1:T(2,128)} %param.14) | copy-start | bytes 580
  5.7 13.8 %collective-permute-start = (f32[5,16,24,1]{2,1,3,0:T(8,128)S(1)}, f32[5,16,24,1]{2,1,3,0:T(8,128)}, u32[]{:S(2)}, u32[]{:S(2)}) collective-permute-start(f32[5,16,24,1]{2,1,3,0:T(8,128)S(1)} %copy.57), channel_id=1, source_target_pairs={{0,8},{8,16},{16,24},{24,0},{1,9},{9,17},{17,25},{25,1},{2,10},{10... | collective-permute-start | bytes 23048 | tf_op jit(solution)/shard_map/ppermute | solution.py:18
  7.9 16.1 %collective-permute-start.1 = (f32[5,16,24,1]{2,1,3,0:T(8,128)S(1)}, f32[5,16,24,1]{2,1,3,0:T(8,128)}, u32[]{:S(2)}, u32[]{:S(2)}) collective-permute-start(f32[5,16,24,1]{2,1,3,0:T(8,128)S(1)} %copy.59), channel_id=1, source_target_pairs={{8,0},{16,8},{24,16},{0,24},{9,1},{17,9},{25,17},{1,25},{10,2},{18... | collective-permute-start | bytes 23048 | tf_op jit(solution)/shard_map/ppermute | solution.py:19
  10.8 18.3 %collective-permute-start.2 = (f32[5,16,1,384]{3,1,2,0:T(8,128)}, f32[5,16,1,384]{3,1,2,0:T(8,128)}, u32[]{:S(2)}, u32[]{:S(2)}) collective-permute-start(f32[5,16,1,384]{3,1,2,0:T(8,128)} %copy.61), channel_id=1, source_target_pairs={{0,1},{1,2},{2,3},{3,4},{4,5},{5,6},{6,7},{8,9},{9,10},{10,11},{11... | collective-permute-start | bytes 368648 | tf_op jit(solution)/shard_map/ppermute | solution.py:18
  16.3 14.1 %collective-permute-start.3 = (f32[5,16,1,384]{3,1,2,0:T(8,128)}, f32[5,16,1,384]{3,1,2,0:T(8,128)}, u32[]{:S(2)}, u32[]{:S(2)}) collective-permute-start(f32[5,16,1,384]{3,1,2,0:T(8,128)} %copy.63), channel_id=1, source_target_pairs={{1,0},{2,1},{3,2},{4,3},{5,4},{6,5},{7,6},{9,8},{10,9},{11,10},{12... | collective-permute-start | bytes 368648 | tf_op jit(solution)/shard_map/ppermute | solution.py:19
  18.0 0.6 copy-start.9
  26.3 3.8 %copy-start.4 = (f32[16,24,384]{2,1,0:T(8,128)S(1)}, f32[16,24,384]{2,1,0:T(8,128)}, u32[]{:S(2)}) copy-start(f32[16,24,384]{2,1,0:T(8,128)} %param.11) | copy-start | bytes 1769476
  30.1 1.3 copy-start.8
  34.9 32.1 %all-to-all-start = ((f32[4,384,384]{2,1,0:T(8,128)}), f32[4,384,384]{2,1,0:T(8,128)S(1)}, u32[]{:S(2)}, u32[]{:S(2)}) async-start(f32[4,384,384]{2,1,0:T(8,128)} %bitcast.68), calls=%async_computation | async-start | bytes 4718592 | tf_op jit(solution)/shard_map/all_to_all | solution.py:72
  67.0 40.3 %all-to-all-start.2 = ((s32[8,1,12]{2,1,0:T(1,128)}), s32[8,1,12]{2,1,0:T(1,128)S(1)}, u32[]{:S(2)}, u32[]{:S(2)}) async-start(s32[8,1,12]{2,1,0:T(1,128)} %copy.70), calls=%async_computation.2 | async-start | bytes 8192 | tf_op jit(solution)/shard_map/all_to_all | solution.py:103
  79.6 14.8 %copy-start.1 = (f32[24,64,1536]{2,1,0:T(8,128)S(1)}, f32[24,64,1536]{2,1,0:T(8,128)}, u32[]{:S(2)}) copy-start(f32[24,64,1536]{2,1,0:T(8,128)} %add_select_fusion) | copy-start | bytes 28311556
  107.3 33.1 %all-to-all-start.1 = ((f32[384,4,384]{2,0,1:T(8,128)}), f32[384,4,384]{2,0,1:T(8,128)}, u32[]{:S(2)}, u32[]{:S(2)}) async-start(f32[384,4,384]{2,0,1:T(8,128)} %fusion.31), calls=%async_computation.1 | async-start | bytes 4718592 | tf_op jit(solution)/shard_map/all_to_all | solution.py:83
  140.4 6.3 %copy-start.10 = (s32[48]{0:T(128)S(1)}, s32[48]{0:T(128)}, u32[]{:S(2)}) copy-start(s32[48]{0:T(128)} %copy-done.9) | copy-start | bytes 580
  140.4 6.4 %copy-start.6 = (f32[24,2]{0,1:T(2,128)S(1)}, f32[24,2]{0,1:T(2,128)}, u32[]{:S(2)}) copy-start(f32[24,2]{0,1:T(2,128)} %param.15) | copy-start | bytes 580
  140.4 6.4 %copy-start.2 = (f32[4,16,24,384]{3,2,1,0:T(8,128)S(1)}, f32[4,16,24,384]{3,2,1,0:T(8,128)}, u32[]{:S(2)}) copy-start(f32[4,16,24,384]{3,2,1,0:T(8,128)} %fusion.4) | copy-start | bytes 7077892
  140.4 211.6 %all-to-all-start.3 = ((f32[8,12,4,16,384]{4,3,2,1,0:T(8,128)}), f32[8,12,4,16,384]{4,3,2,1,0:T(8,128)}, u32[]{:S(2)}, u32[]{:S(2)}) async-start(f32[8,12,4,16,384]{4,3,2,1,0:T(8,128)} %bitcast.67), calls=%async_computation.3 | async-start | bytes 18874368 | tf_op jit(solution)/shard_map/all_to_all | solution.py:106
